TPU v7x, 128 devices: a whole 4x4x4 slice. The times are simulated.
128 devices in a mesh: req: 8 (over x, core), kv: 16 (over y, z).
Axes of the slice: x: 4, y: 4, z: 4, core: 2. Of those that a mesh axis runs over, the one named last changes fastest.
Arguments:
- x_steps: bfloat16 [4, 1024, 1536], P(None, ('req', 'kv')), may hold values from -6 to 6
- lengths: int32 [128], replicated, may hold values from 16 to 8192
- perm: int32 [128], replicated, may hold values from 0 to 127, as said below
- parents: int32 [4, 1024], replicated, may hold values from 0 to 7
- table: int32 [1024, 9], P(('req', 'kv')), may hold values from 0 to 9215, as said below
- pool: bfloat16 [9216, 128, 256], P(('req', 'kv')), may hold values from -900 to 900
- norm_attn: float32 [1536], replicated, may hold values from 0.1 to 1.9
- w_query: bfloat16 [1536, 1536], replicated, may hold values from -0.15625 to 0.15625
- w_keyval: bfloat16 [1536, 256], replicated, may hold values from -0.15625 to 0.15625
- w_out: bfloat16 [1536, 1536], replicated, may hold values from -0.15625 to 0.15625
- norm_mlp: float32 [1536], replicated, may hold values from 0.1 to 1.9
- w_gate: bfloat16 [1536, 4608], P(None, 'kv'), may hold values from -0.15625 to 0.15625
- w_up: bfloat16 [1536, 4608], P(None, 'kv'), may hold values from -0.15625 to 0.15625
- w_down: bfloat16 [4608, 1536], P('kv'), may hold values from -0.09375 to 0.09375
Outputs:
- outputs: bfloat16 [4, 1024, 1536], P(None, ('req', 'kv'))
Inputs may be any that keep to these rules, and one draw needn't show every extreme that they name: perm is a permutation with perm[s] % 16 == s % 16; among the 8 slots s with one s // 16 and one s % 16 // 8, every req index occurs as perm[s] // 16 exactly once. The entries of row b lie in [(b // 8) * 72, (b // 8 + 1) * 72); no page appears twice in the table.
All inputs are finite; a program needn't handle non-finite values.
Results may differ from a plain program's by a relative error of at most 0.02.
Values may be sent and summed in bfloat16 or wider, within the bound.
No kernel may reach another device: no remote copies, remote signals or barrier semaphores. Data moves between devices by JAX's collectives and lax.ppermute only.
A program may use at most 192 MiB of HBM per device.

v0:
```python
import jax
import jax.numpy as jnp
from jax import lax
from jax.sharding import PartitionSpec as P

WINDOW = 1024
PAGE = 128
BEAMS = 8
EPSILON = 1e-06
NEGATIVE = -1e30


def merged_2(array, axis, combine):
    everything = jax.tree.map(lambda part: lax.all_gather(part, axis), array)
    first = jax.tree.map(lambda part: part[0], everything)

    def turn(k, so_far):
        return combine(so_far, jax.tree.map(lambda part: part[k], everything))

    return lax.fori_loop(1, lax.axis_size(axis), turn, first)


def member_of(beam_index, half_index, halves):
    return beam_index % 2 + 2 * half_index + 2 * halves * (beam_index // 2)


def rms_round(values, gain):
    wide = values.astype(jnp.float32)
    mean_square = jnp.mean(wide * wide, axis=-1, keepdims=True)
    return (wide * lax.rsqrt(mean_square + EPSILON) * gain).astype(jnp.bfloat16)


def page_partial(queries, pages, key_pos, length, step_index):
    head_dim = queries.shape[-1]
    keys = pages[:, :, :head_dim]
    values = pages[:, :, head_dim:]
    scores = jnp.einsum(
        "jrhd,rkd->jrhk", queries, keys, preferred_element_type=jnp.float32
    ) * head_dim ** (-0.5)
    allowed = (key_pos < length[:, None]) & (key_pos > length[:, None] + step_index - WINDOW)
    scores = jnp.where(allowed[None, :, None, :], scores, NEGATIVE)
    highest = jnp.max(scores, axis=-1)
    weights = jnp.exp(scores - highest[..., None]).astype(jnp.bfloat16)
    totals = jnp.sum(weights.astype(jnp.float32), axis=-1)
    weighted = jnp.einsum("jrhk,rkd->jrhd", weights, values, preferred_element_type=jnp.float32)
    return (highest, totals, weighted)


def fresh_partial(queries, entries, count):
    head_dim = queries.shape[-1]
    keys = entries[..., :count, :head_dim]
    values = entries[..., :count, head_dim:]
    scores = jnp.einsum(
        "...hd,...kd->...hk", queries, keys, preferred_element_type=jnp.float32
    ) * head_dim ** (-0.5)
    highest = jnp.max(scores, axis=-1)
    weights = jnp.exp(scores - highest[..., None]).astype(jnp.bfloat16)
    totals = jnp.sum(weights.astype(jnp.float32), axis=-1)
    weighted = jnp.einsum("...hk,...kd->...hd", weights, values, preferred_element_type=jnp.float32)
    return (highest, totals, weighted)


def join_parts(first, second):
    highest = jnp.maximum(first[0], second[0])
    scale_first = jnp.exp(first[0] - highest)
    scale_second = jnp.exp(second[0] - highest)
    totals = first[1] * scale_first + second[1] * scale_second
    weighted = first[2] * scale_first[..., None] + second[2] * scale_second[..., None]
    return (highest, totals, weighted)


def feed_forward(mlp_in, w_gate, w_up, w_down):
    gate = jnp.dot(mlp_in, w_gate, preferred_element_type=jnp.float32)
    upward = jnp.dot(mlp_in, w_up, preferred_element_type=jnp.float32)
    hidden = (jax.nn.gelu(gate, approximate=True) * upward).astype(jnp.bfloat16)
    return jnp.dot(hidden, w_down, preferred_element_type=jnp.float32)


def rank_within(labels, offsets):
    earlier = (labels[None, :] == labels[:, None]) & (offsets[None, :] < offsets[:, None])
    return jnp.sum(earlier.astype(jnp.int32), axis=1)


def pick_half(array, halves, half):
    shaped = array.reshape((BEAMS // 2, halves, 2) + array.shape[1:])
    picked = lax.dynamic_index_in_dim(shaped, half, 1, keepdims=False)
    return picked.reshape((BEAMS,) + array.shape[1:])


def place_block(block, filler, halves, half):
    whole = jnp.full((BEAMS // 2, halves, 2) + block.shape[1:], filler, block.dtype)
    placed = lax.dynamic_update_slice_in_dim(
        whole, block.reshape((BEAMS // 2, 1, 2) + block.shape[1:]), half, 1
    )
    return placed.reshape((BEAMS * halves,) + block.shape[1:])


def on_device(
    x_steps,
    lengths,
    perm,
    parents,
    table,
    pool,
    norm_attn,
    w_query,
    w_keyval,
    w_out,
    norm_mlp,
    w_gate,
    w_up,
    w_down,
):
    steps, rows, width = x_steps.shape
    head_dim = pool.shape[2] // 2
    heads = w_query.shape[1] // head_dim
    span = table.shape[1] * pool.shape[1]
    req_count = lax.axis_size("req")
    kv_count = lax.axis_size("kv")
    group = lax.axis_index("req")
    member = lax.axis_index("kv")
    halves = kv_count // BEAMS
    half = member // 2 % halves
    beam = member % 2 + 2 * (member // (2 * halves))
    per_group = halves * rows
    group_rows = kv_count * rows
    quota = rows // req_count
    offsets = jnp.arange(rows, dtype=jnp.int32)
    slot_ids = group * per_group + half * rows + offsets
    placed = lax.dynamic_slice_in_dim(perm.reshape(req_count, per_group), half * rows, rows, 1)
    serving = lax.dynamic_index_in_dim(placed, group, 0, keepdims=False)
    target = jnp.sum(
        jnp.where(placed == slot_ids[None, :], jnp.arange(req_count, dtype=jnp.int32)[:, None], 0),
        axis=0,
    )
    anchor = serving // per_group
    send_order = jnp.argsort(target * rows + offsets)
    outgoing = x_steps[:, send_order].reshape(steps, req_count, quota, width)
    arrived = lax.all_to_all(outgoing, "req", split_axis=1, concat_axis=1, tiled=True).reshape(
        steps, rows, width
    )
    inputs = arrived[:, anchor * quota + rank_within(anchor, offsets)]
    length = lengths[serving]
    first_page = jnp.maximum(length - WINDOW + 1, 0) // PAGE
    key_pos = first_page[:, None] * PAGE + jnp.arange(span, dtype=jnp.int32)[None, :]
    device = group * kv_count + member
    pages = pool[table - device * pool.shape[0]].reshape(rows, span, 2 * head_dim)
    family = lax.dynamic_slice_in_dim(parents, group * group_rows, group_rows, 1)
    row_ids = jnp.arange(group_rows, dtype=jnp.int32)
    row_member = row_ids // rows
    row_half = row_member // 2 % halves
    within = row_ids % rows
    ancestor = row_member % 2 + 2 * (row_member // (2 * halves))
    recent = jnp.zeros((group_rows, steps, 2 * head_dim), jnp.bfloat16)
    results = []
    for step_index in range(steps):
        parent_rows = member_of(family[step_index], row_half, halves) * rows + within
        ancestor = ancestor[parent_rows]
        recent = recent[parent_rows]
        current = inputs[step_index]
        normed = rms_round(current, norm_attn)
        query = jnp.dot(normed, w_query, preferred_element_type=jnp.float32).astype(jnp.bfloat16)
        fresh = jnp.dot(normed, w_keyval, preferred_element_type=jnp.float32).astype(jnp.bfloat16)
        query_all, fresh_all = (
            lax.all_gather(query, "kv", axis=0, tiled=True),
            lax.all_gather(fresh, "kv", axis=0, tiled=True),
        )
        recent = recent.at[:, step_index].set(fresh_all)
        query_block = pick_half(query_all.reshape(kv_count, rows, heads, head_dim), halves, half)
        held = pick_half(ancestor.reshape(kv_count, rows), halves, half) == beam
        page = page_partial(query_block, pages, key_pos, length, step_index)
        held_heads = held[..., None]
        highest = place_block(jnp.where(held_heads, page[0], NEGATIVE), NEGATIVE, halves, half)
        totals = place_block(jnp.where(held_heads, page[1], 0.0), 0.0, halves, half)
        weighted = place_block(jnp.where(held_heads[..., None], page[2], 0.0), 0.0, halves, half)
        merged = merged_2((highest, totals, weighted), "kv", join_parts)
        page_own = tuple(
            (
                lax.dynamic_index_in_dim(member_part, member, 0, keepdims=False)
                for member_part in merged
            )
        )
        own_entries = lax.dynamic_slice_in_dim(recent, member * rows, rows, 0)
        joined = join_parts(
            page_own,
            fresh_partial(query.reshape(rows, heads, head_dim), own_entries, step_index + 1),
        )
        attended = (
            (joined[2] / joined[1][..., None]).astype(jnp.bfloat16).reshape(rows, heads * head_dim)
        )
        residual = (
            current.astype(jnp.float32)
            + jnp.dot(attended, w_out, preferred_element_type=jnp.float32)
        ).astype(jnp.bfloat16)
        terms = feed_forward(
            lax.all_gather(rms_round(residual, norm_mlp), "kv", axis=0, tiled=True),
            w_gate,
            w_up,
            w_down,
        )
        summed = lax.psum_scatter(
            terms.astype(jnp.bfloat16), "kv", scatter_dimension=0, tiled=True
        ).astype(jnp.float32)
        results.append((residual.astype(jnp.float32) + summed).astype(jnp.bfloat16))
    finished = jnp.stack(results)
    back_order = jnp.argsort(anchor * rows + offsets)
    leaving = finished[:, back_order].reshape(steps, req_count, quota, width)
    returned = lax.all_to_all(leaving, "req", split_axis=1, concat_axis=1, tiled=True).reshape(
        steps, rows, width
    )
    return returned[:, target * quota + rank_within(target, offsets)]


def solution(mesh):
    in_specs = (
        P(None, ("req", "kv"), None),
        P(),
        P(),
        P(),
        P(("req", "kv"), None),
        P(("req", "kv"), None, None),
        P(),
        P(),
        P(),
        P(),
        P(),
        P(None, "kv"),
        P(None, "kv"),
        P("kv", None),
    )
    out_specs = P(None, ("req", "kv"), None)
    return jax.shard_map(
        on_device, mesh=mesh, in_specs=in_specs, out_specs=out_specs, check_vma=False
    )
```

profile of v0, /device:TPU:1, one launch (start us, length us, event | category | flops | bytes accessed | tf_op | source)
XLA Modules:
  0.0 938.8 jit_solution(8522241222401222963)
XLA Ops:
  39.0 20.2 %all_gather.90 = bf16[128,1536]{1,0:T(8,128)(2,1)S(1)} all-gather(bf16[8,1536]{1,0:T(8,128)(2,1)S(1)} %convolution_convert_fusion.4), channel_id=1, replica_groups=mesh['req'=8,'kv'=16] {'kv'}, dimensions={0}, use_global_device_ids=true | all-gather | bytes 417792 | tf_op jit(solution)/shard_map/all_gather | solution.py:165
  67.1 19.5 %all_gather.72 = bf16[128,1536]{1,0:T(8,128)(2,1)S(1)} all-gather(bf16[8,1536]{1,0:T(8,128)(2,1)S(1)} %convolution_convert_fusion.7), channel_id=1, replica_groups=mesh['req'=8,'kv'=16] {'kv'}, dimensions={0}, use_global_device_ids=true | all-gather | bytes 417792 | tf_op jit(solution)/shard_map/all_gather | solution.py:165
  96.3 17.8 %all_gather.78 = bf16[128,1536]{1,0:T(8,128)(2,1)S(1)} all-gather(bf16[8,1536]{1,0:T(8,128)(2,1)S(1)} %convolution_convert_fusion.6), channel_id=1, replica_groups=mesh['req'=8,'kv'=16] {'kv'}, dimensions={0}, use_global_device_ids=true | all-gather | bytes 417792 | tf_op jit(solution)/shard_map/all_gather | solution.py:165
  125.7 20.9 %all_gather.76 = bf16[128,256]{1,0:T(8,128)(2,1)S(1)} all-gather(bf16[8,256]{1,0:T(8,128)(2,1)S(1)} %convolution_convert_fusion.11), channel_id=1, replica_groups=mesh['req'=8,'kv'=16] {'kv'}, dimensions={0}, use_global_device_ids=true | all-gather | bytes 69632 | tf_op jit(solution)/shard_map/all_gather | solution.py:166
  149.5 16.4 %all_gather.82 = bf16[128,256]{1,0:T(8,128)(2,1)S(1)} all-gather(bf16[8,256]{1,0:T(8,128)(2,1)S(1)} %convolution_convert_fusion.10), channel_id=1, replica_groups=mesh['req'=8,'kv'=16] {'kv'}, dimensions={0}, use_global_device_ids=true | all-gather | bytes 69632 | tf_op jit(solution)/shard_map/all_gather | solution.py:166
  168.9 19.8 %all_gather.88 = bf16[128,256]{1,0:T(8,128)(2,1)S(1)} all-gather(bf16[8,256]{1,0:T(8,128)(2,1)S(1)} %convolution_convert_fusion.9), channel_id=1, replica_groups=mesh['req'=8,'kv'=16] {'kv'}, dimensions={0}, use_global_device_ids=true | all-gather | bytes 69632 | tf_op jit(solution)/shard_map/all_gather | solution.py:166
  191.6 16.4 %all_gather.94 = bf16[128,256]{1,0:T(8,128)(2,1)S(1)} all-gather(bf16[8,256]{1,0:T(8,128)(2,1)S(1)} %convolution_convert_fusion.8), channel_id=1, replica_groups=mesh['req'=8,'kv'=16] {'kv'}, dimensions={0}, use_global_device_ids=true | all-gather | bytes 69632 | tf_op jit(solution)/shard_map/all_gather | solution.py:166
  218.9 21.9 %all_gather.84 = bf16[128,1536]{1,0:T(8,128)(2,1)S(1)} all-gather(bf16[8,1536]{1,0:T(8,128)(2,1)S(1)} %convolution_convert_fusion.5), channel_id=1, replica_groups=mesh['req'=8,'kv'=16] {'kv'}, dimensions={0}, use_global_device_ids=true | all-gather | bytes 417792 | tf_op jit(solution)/shard_map/all_gather | solution.py:165
  248.8 20.0 %all_gather.91 = f32[16,16,8,12]{1,2,3,0:T(8,128)} all-gather(f32[1,16,8,12]{1,2,3,0:T(8,128)S(1)} %copy.375), channel_id=1, replica_groups=mesh['req'=8,'kv'=16] {'kv'}, dimensions={0}, use_global_device_ids=true | all-gather | bytes 104448 | tf_op jit(solution)/shard_map/all_gather | solution.py:14
  268.8 22.4 %all_gather.92 = f32[16,16,8,12]{1,2,3,0:T(8,128)} all-gather(f32[1,16,8,12]{1,2,3,0:T(8,128)S(1)} %copy.378), channel_id=1, replica_groups=mesh['req'=8,'kv'=16] {'kv'}, dimensions={0}, use_global_device_ids=true | all-gather | bytes 104448 | tf_op jit(solution)/shard_map/all_gather | solution.py:14
  291.2 20.8 %all_gather.73 = f32[16,16,8,12]{1,2,3,0:T(8,128)S(1)} all-gather(f32[1,16,8,12]{1,2,3,0:T(8,128)S(1)} %copy.320), channel_id=1, replica_groups=mesh['req'=8,'kv'=16] {'kv'}, dimensions={0}, use_global_device_ids=true | all-gather | bytes 104448 | tf_op jit(solution)/shard_map/all_gather | solution.py:14
  312.0 22.6 %all_gather.74 = f32[16,16,8,12]{1,2,3,0:T(8,128)S(1)} all-gather(f32[1,16,8,12]{1,2,3,0:T(8,128)S(1)} %copy.323), channel_id=1, replica_groups=mesh['req'=8,'kv'=16] {'kv'}, dimensions={0}, use_global_device_ids=true | all-gather | bytes 104448 | tf_op jit(solution)/shard_map/all_gather | solution.py:14
  334.6 21.6 %all_gather.79 = f32[16,16,8,12]{1,2,3,0:T(8,128)S(1)} all-gather(f32[1,16,8,12]{1,2,3,0:T(8,128)S(1)} %copy.341), channel_id=1, replica_groups=mesh['req'=8,'kv'=16] {'kv'}, dimensions={0}, use_global_device_ids=true | all-gather | bytes 104448 | tf_op jit(solution)/shard_map/all_gather | solution.py:14
  356.3 18.0 %all_gather.80 = f32[16,16,8,12]{1,2,3,0:T(8,128)S(1)} all-gather(f32[1,16,8,12]{1,2,3,0:T(8,128)S(1)} %copy.344), channel_id=1, replica_groups=mesh['req'=8,'kv'=16] {'kv'}, dimensions={0}, use_global_device_ids=true | all-gather | bytes 104448 | tf_op jit(solution)/shard_map/all_gather | solution.py:14
  374.3 19.4 %all_gather.85 = f32[16,16,8,12]{1,2,3,0:T(8,128)} all-gather(f32[1,16,8,12]{1,2,3,0:T(8,128)S(1)} %copy.358), channel_id=1, replica_groups=mesh['req'=8,'kv'=16] {'kv'}, dimensions={0}, use_global_device_ids=true | all-gather | bytes 104448 | tf_op jit(solution)/shard_map/all_gather | solution.py:14
  393.7 20.4 %all_gather.86 = f32[16,16,8,12]{1,2,3,0:T(8,128)} all-gather(f32[1,16,8,12]{1,2,3,0:T(8,128)S(1)} %copy.361), channel_id=1, replica_groups=mesh['req'=8,'kv'=16] {'kv'}, dimensions={0}, use_global_device_ids=true | all-gather | bytes 104448 | tf_op jit(solution)/shard_map/all_gather | solution.py:14
  426.7 46.2 %while.83 = (s32[]{:T(128)}, f32[16,8,12]{0,1,2:T(8,128)S(1)}, f32[16,8,12]{0,1,2:T(8,128)S(1)}, f32[16,8,12,128]{3,2,1,0:T(8,128)S(1)}, f32[16,16,8,12]{1,2,3,0...) while((s32[]{:T(128)}, f32[16,8,12]{0,1,2:T(8,128)S(1)}, ...), condition=%wide.region_32.33_spmd, body=%wide.region_31.32_spmd.sunk | while | flops 599045 | bytes 4018327 | solution.py:20
  475.2 46.3 %while.80 = (s32[]{:T(128)}, f32[16,8,12]{0,1,2:T(8,128)S(1)}, f32[16,8,12]{0,1,2:T(8,128)S(1)}, f32[16,8,12,128]{3,2,1,0:T(8,128)S(1)}, f32[16,16,8,12]{1,2,3,0...) while((s32[]{:T(128)}, f32[16,8,12]{0,1,2:T(8,128)S(1)}, ...), condition=%wide.region_7.8_spmd, body=%wide.region_6.7_spmd.sunk | while | flops 599045 | bytes 4018327 | solution.py:20
  524.6 73.6 %while.81 = (s32[]{:T(128)}, f32[16,8,12]{0,1,2:T(8,128)S(1)}, f32[16,8,12]{0,1,2:T(8,128)S(1)}, f32[16,8,12,128]{3,2,1,0:T(8,128)}, f32[16,16,8,12]{1,2,3,0:T(8...) while((s32[]{:T(128)}, f32[16,8,12]{0,1,2:T(8,128)S(1)}, ...), condition=%wide.region_14.15_spmd, body=%wide.region_13.14_spmd.sunk | while | flops 599045 | bytes 4018327 | solution.py:20
  610.3 46.2 %while.82 = (s32[]{:T(128)}, f32[16,8,12]{0,1,2:T(8,128)S(1)}, f32[16,8,12]{0,1,2:T(8,128)S(1)}, f32[16,8,12,128]{3,2,1,0:T(8,128)S(1)}, f32[16,16,8,12]{1,2,3,0...) while((s32[]{:T(128)}, f32[16,8,12]{0,1,2:T(8,128)S(1)}, ...), condition=%wide.region_23.24_spmd, body=%wide.region_22.23_spmd.sunk | while | flops 599045 | bytes 4018327 | solution.py:20
  661.8 16.6 %all_gather.95 = bf16[128,1536]{1,0:T(8,128)(2,1)S(1)} all-gather(bf16[8,1536]{1,0:T(8,128)(2,1)S(1)} %get-tuple-element.991), channel_id=1, replica_groups=mesh['req'=8,'kv'=16] {'kv'}, dimensions={0}, use_global_device_ids=true | all-gather | bytes 417792 | tf_op jit(solution)/shard_map/all_gather | solution.py:196
  678.4 17.7 %all_gather.89 = bf16[128,1536]{1,0:T(8,128)(2,1)S(1)} all-gather(bf16[8,1536]{1,0:T(8,128)(2,1)S(1)} %get-tuple-element.990), channel_id=1, replica_groups=mesh['req'=8,'kv'=16] {'kv'}, dimensions={0}, use_global_device_ids=true | all-gather | bytes 417792 | tf_op jit(solution)/shard_map/all_gather | solution.py:196
  722.6 17.9 %all_gather.77 = bf16[128,1536]{1,0:T(8,128)(2,1)S(1)} all-gather(bf16[8,1536]{1,0:T(8,128)(2,1)S(1)} %copy-done.28), channel_id=1, replica_groups=mesh['req'=8,'kv'=16] {'kv'}, dimensions={0}, use_global_device_ids=true | all-gather | bytes 417792 | tf_op jit(solution)/shard_map/all_gather | solution.py:196
  744.1 170.9 %all-reduce.7.cloned.1.call-done = (bf16[128,1536]{1,0:T(8,128)(2,1)}, bf16[128,1536]{1,0:T(8,128)(2,1)}, bf16[128,1536]{1,0:T(8,128)(2,1)}, bf16[128,1536]{1,0:T(8,128)(2,1)}) async-done(((bf16[128,1536]{1,0:T(8,128)(2,1)}, bf16[128,1536]{1,0:T(8,128)(2,1)}, bf16[128,1536]{1,0:T(8,128)(2,1)}, bf16[128,1536]{1,0:T(8,128)(2,1)}), (bf16[128,1536]{1,0:T(8,128)(2,1)}, bf16[128,1536]{1,0:T(8,128)(2,1)}, ...) | async-done | bytes 1572880
  (636 shorter events, 380.3 us)
Async XLA Ops:
  6.5 691.6 %copy-start = (bf16[288,1536]{1,0:T(8,128)(2,1)S(1)}, bf16[288,1536]{1,0:T(8,128)(2,1)}, u32[]{:S(2)}) copy-start(bf16[288,1536]{1,0:T(8,128)(2,1)} %param.43) | copy-start | bytes 2654212
  12.4 22.5 %all-to-all-start = ((bf16[4,8,1,1536]{3,0,2,1:T(4,128)(2,1)}), bf16[4,8,1,1536]{3,0,2,1:T(4,128)(2,1)S(1)}, u32[]{:S(2)}, u32[]{:S(2)}) async-start(bf16[4,8,1,1536]{3,0,2,1:T(4,128)(2,1)} %copy.313), calls=%async_computation | async-start | bytes 196608 | tf_op jit(solution)/shard_map/all_to_all | solution.py:139
  18.2 407.1 %all-gather.11.cloned.1.call-start = ((), (), s32[]{:S(2)}) async-start(), calls=%async_computation.5 | async-start | bytes 13369344 | tf_op jit(solution)/shard_map/all_gather | solution.py:14
  63.7 409.4 %all-gather.5.cloned.1.call-start = ((), (), s32[]{:S(2)}) async-start(), calls=%async_computation.2 | async-start | bytes 13369344 | tf_op jit(solution)/shard_map/all_gather | solution.py:14
  92.9 429.2 %all-gather.7.cloned.1.call-start = ((), (), s32[]{:S(2)}) async-start(), calls=%async_computation.3 | async-start | bytes 13369344 | tf_op jit(solution)/shard_map/all_gather | solution.py:14
  120.4 488.5 %all-gather.9.cloned.1.call-start = ((), (), s32[]{:S(2)}) async-start(), calls=%async_computation.4 | async-start | bytes 13369344 | tf_op jit(solution)/shard_map/all_gather | solution.py:14
  167.8 246.9 %copy-start.21 = (bf16[128,4,256]{2,1,0:T(4,128)(2,1)}, bf16[128,4,256]{2,1,0:T(4,128)(2,1)S(1)}, u32[]{:S(2)}) copy-start(bf16[128,4,256]{2,1,0:T(4,128)(2,1)S(1)} %scatter.15) | copy-start | bytes 786436
  190.5 226.4 %copy-start.20 = (bf16[128,4,256]{2,1,0:T(4,128)(2,1)}, bf16[128,4,256]{2,1,0:T(4,128)(2,1)S(1)}, u32[]{:S(2)}) copy-start(bf16[128,4,256]{2,1,0:T(4,128)(2,1)S(1)} %scatter.16) | copy-start | bytes 786436
  248.7 169.2 %copy-start.27 = (bf16[128,4,256]{2,1,0:T(4,128)(2,1)}, bf16[128,4,256]{2,1,0:T(4,128)(2,1)S(1)}, u32[]{:S(2)}) copy-start(bf16[128,4,256]{2,1,0:T(4,128)(2,1)S(1)} %scatter.19) | copy-start | bytes 786436
  248.8 171.7 %copy-start.11 = (f32[8,1152,8,12]{1,3,2,0:T(8,128)S(1)}, f32[8,1152,8,12]{1,3,2,0:T(8,128)}, u32[]{:S(2)}) copy-start(f32[8,1152,8,12]{1,3,2,0:T(8,128)} %copy-done.10) | copy-start | bytes 10616836
  312.0 107.6 %copy-start.18 = (f32[16,16,8,12]{1,2,3,0:T(8,128)}, f32[16,16,8,12]{1,2,3,0:T(8,128)S(1)}, u32[]{:S(2)}) copy-start(f32[16,16,8,12]{1,2,3,0:T(8,128)S(1)} %all_gather.73) | copy-start | bytes 294916
  334.6 85.0 %copy-start.19 = (f32[16,16,8,12]{1,2,3,0:T(8,128)}, f32[16,16,8,12]{1,2,3,0:T(8,128)S(1)}, u32[]{:S(2)}) copy-start(f32[16,16,8,12]{1,2,3,0:T(8,128)S(1)} %all_gather.74) | copy-start | bytes 294916
  356.3 62.5 %copy-start.16 = (f32[16,16,8,12]{1,2,3,0:T(8,128)}, f32[16,16,8,12]{1,2,3,0:T(8,128)S(1)}, u32[]{:S(2)}) copy-start(f32[16,16,8,12]{1,2,3,0:T(8,128)S(1)} %all_gather.79) | copy-start | bytes 294916
  424.4 490.5 %all-reduce.7.cloned.1.call-start = ((), (), s32[]{:S(2)}) async-start(), calls=%async_computation.6 | async-start | bytes 3145728
  475.2 46.6 %copy-start.40 = (f32[8,1,12]{2,1,0:T(1,128)S(1)}, f32[8,1,12]{2,1,0:T(1,128)}, u32[]{:S(2)}) copy-start(f32[8,1,12]{2,1,0:T(1,128)} %fusion.132) | copy-start | bytes 1156
  524.5 73.9 %copy-start.34 = (f32[8,12]{1,0:T(8,128)S(1)}, f32[8,12]{1,0:T(8,128)}, u32[]{:S(2)}) copy-start(f32[8,12]{1,0:T(8,128)} %copy-done.33) | copy-start | bytes 1156
  524.5 73.9 %copy-start.35 = (f32[8,12]{1,0:T(8,128)S(1)}, f32[8,12]{1,0:T(8,128)}, u32[]{:S(2)}) copy-start(f32[8,12]{1,0:T(8,128)} %convert_reduce_fusion.6) | copy-start | bytes 1156
  608.8 52.2 %copy-start.23 = (f32[8,1536]{1,0:T(8,128)}, f32[8,1536]{1,0:T(8,128)S(1)}, u32[]{:S(2)}) copy-start(f32[8,1536]{1,0:T(8,128)S(1)} %get-tuple-element.1037) | copy-start | bytes 147460
  610.2 46.5 %copy-start.30 = (f32[8,12]{1,0:T(8,128)S(1)}, f32[8,12]{1,0:T(8,128)}, u32[]{:S(2)}) copy-start(f32[8,12]{1,0:T(8,128)} %copy-done.29) | copy-start | bytes 1156
  610.2 46.5 %copy-start.31 = (f32[8,12]{1,0:T(8,128)S(1)}, f32[8,12]{1,0:T(8,128)}, u32[]{:S(2)}) copy-start(f32[8,12]{1,0:T(8,128)} %convert_reduce_fusion.5) | copy-start | bytes 1156
  661.8 58.5 %copy-start.3 = (bf16[1536,288]{0,1:T(8,128)(2,1)S(1)}, bf16[1536,288]{0,1:T(8,128)(2,1)}, u32[]{:S(2)}) copy-start(bf16[1536,288]{0,1:T(8,128)(2,1)} %param.41) | copy-start | bytes 2654212
  720.7 194.2 %copy-start.24 = (f32[8,1536]{1,0:T(8,128)S(1)}, f32[8,1536]{1,0:T(8,128)}, u32[]{:S(2)}) copy-start(f32[8,1536]{1,0:T(8,128)} %copy-done.23) | copy-start | bytes 147460
  720.7 195.0 %copy-start.26 = (f32[8,1536]{1,0:T(8,128)S(1)}, f32[8,1536]{1,0:T(8,128)}, u32[]{:S(2)}) copy-start(f32[8,1536]{1,0:T(8,128)} %copy-done.25) | copy-start | bytes 147460
  919.3 11.4 %all-to-all-start.1 = ((bf16[4,8,1,1536]{3,0,2,1:T(4,128)(2,1)}), bf16[4,8,1,1536]{3,0,2,1:T(4,128)(2,1)S(1)}, u32[]{:S(2)}, u32[]{:S(2)}) async-start(bf16[4,8,1,1536]{3,0,2,1:T(4,128)(2,1)} %bitcast.140), calls=%async_computation.1 | async-start | bytes 196608 | tf_op jit(solution)/shard_map/all_to_all | solution.py:208
  (33 other events, 423.8 us)
Sparse Core Ops, SparseCore 0:
  63.8 97.4 all-gather.10
  163.5 91.9 all-gather.4
  257.7 102.1 all-gather.6
  424.5 152.7 all-gather.8
  742.9 172.0 all-reduce.6
where the time goes:
time: 955 us; the launch traced here: 939 us
  blocking collectives  387 us (41%)
  waiting for transfers between devices  176 us (18%)
  other arithmetic  146 us (15%)
  local copies, waits for them, and re-layouts  144 us (15%)
  matrix products  56.8 us (6%)
  between operations  15.5 us (2%)
  starting transfers between devices  12.6 us (1%)
    unnamed x6, waiting for transfers between devices  171 us
    all_gather x8, blocking collectives, merged_2(): everything = jax.tree.map(lambda part: lax.all_gather(part, axis), array)  165 us
    all_gather x4, blocking collectives, on_device(): lax.all_gather(query, 'kv', axis=0, tiled=True)  79.3 us
    all_gather x4, blocking collectives, on_device(): lax.all_gather(fresh, 'kv', axis=0, tiled=True)  73.6 us
    dynamic_slice x60, local copies, waits for them, and re-layouts, turn(): return combine(so_far, jax.tree.map(lambda part: part[k], everything))  71.7 us
    add x60, other arithmetic, join_parts(): first[2] * scale_first[..., None] + second[2] * scale_second[..., None]  70.3 us
    all_gather x4, blocking collectives, on_device(): lax.all_gather(rms_round(residual, norm_mlp), 'kv', axis=0, tiled=True)  68.5 us
    add x64, other arithmetic, join_parts(): totals = first[1] * scale_first + second[1] * scale_second  53.3 us
  transfers between devices with their start and end apart: 7, of which 2 were waited for; matrix products, arithmetic and copies ran while one was open for 27% of the time, Pallas kernels for 0%

commit v1 on v0

--- a/solution.py
+++ b/solution.py
@@ -8,6 +8,28 @@
 BEAMS = 8
 EPSILON = 1e-06
 NEGATIVE = -1e30
+
+
+def laid_out(blocks, dim):
+    blocks = jnp.moveaxis(blocks, 0, dim)
+    shape = blocks.shape
+    return blocks.reshape(*shape[:dim], shape[dim] * shape[dim + 1], *shape[dim + 2 :])
+
+
+def gather_around(x, axis, dim):
+    devices = lax.axis_size(axis)
+    pairs = [(i, (i + 1) % devices) for i in range(devices)]
+    back = [(b, a) for a, b in pairs]
+    lower, upper = ([], [])
+    for step in range(devices - 1):
+        if step % 2 == 0:
+            lower.append(lax.ppermute(lower[-1] if lower else x, axis, pairs))
+        else:
+            upper.append(lax.ppermute(upper[-1] if upper else x, axis, back))
+    blocks = jnp.stack([*lower[::-1], x, *upper])
+    shift = lax.axis_index(axis) - len(lower)
+    blocks = blocks[(jnp.arange(devices) - shift) % devices]
+    return laid_out(blocks, dim)
 
 
 def merged_2(array, axis, combine):
@@ -193,10 +215,7 @@
             + jnp.dot(attended, w_out, preferred_element_type=jnp.float32)
         ).astype(jnp.bfloat16)
         terms = feed_forward(
-            lax.all_gather(rms_round(residual, norm_mlp), "kv", axis=0, tiled=True),
-            w_gate,
-            w_up,
-            w_down,
+            gather_around(rms_round(residual, norm_mlp), "kv", 0), w_gate, w_up, w_down
         )
         summed = lax.psum_scatter(
             terms.astype(jnp.bfloat16), "kv", scatter_dimension=0, tiled=True

time: 955 us -> 1050 us (1.099)
  starting transfers between devices: 12.6 us -> 87.7 us
  blocking collectives: 387 us -> 318 us
  local copies, waits for them, and re-layouts: 144 us -> 189 us
  waiting for transfers between devices: 176 us -> 219 us
    ppermute x0 -> x60, starting transfers between devices: none -> 75.1 us  [the longest x28 60.4 us: gather_around(): upper.append(lax.ppermute(upper[-1] if upper else x, axis, back))]
    all_gather x4 -> x0, blocking collectives: 68.5 us -> none  [on_device(): lax.all_gather(rms_round(residual, norm_mlp), 'kv', axis=0, tiled=True)]
    ppermute x0 -> x60, waiting for transfers between devices: none -> 44.1 us  [the longest x32 44 us: gather_around(): lower.append(lax.ppermute(lower[-1] if lower else x, axis, pairs))]
    unnamed x101 -> x233, local copies, waits for them, and re-layouts: 9.75 us -> 45.9 us
  transfers between devices with their start and end apart: 7 -> 67, of which waited for: 2 -> 16; matrix products, arithmetic and copies ran while one was open for 27% -> 30% of each run, Pallas kernels for 0% -> 0%
where the time goes in v1:
time: 1050 us; the launch traced here: 1030 us
  blocking collectives  318 us (30%)
  waiting for transfers between devices  219 us (21%)
  local copies, waits for them, and re-layouts  189 us (18%)
  other arithmetic  145 us (14%)
  starting transfers between devices  87.7 us (8%)
  matrix products  56.5 us (5%)
  between operations  16.2 us (2%)
    unnamed x6, waiting for transfers between devices  169 us
    all_gather x8, blocking collectives, merged_2(): everything = jax.tree.map(lambda part: lax.all_gather(part, axis), array)  165 us
    all_gather x4, blocking collectives, on_device(): lax.all_gather(query, 'kv', axis=0, tiled=True)  79.3 us
    all_gather x4, blocking collectives, on_device(): lax.all_gather(fresh, 'kv', axis=0, tiled=True)  73.8 us
    dynamic_slice x60, local copies, waits for them, and re-layouts, turn(): return combine(so_far, jax.tree.map(lambda part: part[k], everything))  71.7 us
    add x60, other arithmetic, join_parts(): first[2] * scale_first[..., None] + second[2] * scale_second[..., None]  69.9 us
    ppermute x28, starting transfers between devices, gather_around(): upper.append(lax.ppermute(upper[-1] if upper else x, axis, back))  60.4 us
    add x64, other arithmetic, join_parts(): totals = first[1] * scale_first + second[1] * scale_second  53.4 us
  transfers between devices with their start and end apart: 67, of which 16 were waited for; matrix products, arithmetic and copies ran while one was open for 30% of the time, Pallas kernels for 0%

profile of v1, /device:TPU:1, one launch (start us, length us, event | category | flops | bytes accessed | tf_op | source)
XLA Modules:
  0.0 1032.6 jit_solution(3752892807774124084)
XLA Ops:
  12.5 5.8 all-to-all-start
  27.1 7.8 gather_fusion.4
  39.2 20.2 %all_gather.75 = bf16[128,1536]{1,0:T(8,128)(2,1)S(1)} all-gather(bf16[8,1536]{1,0:T(8,128)(2,1)S(1)} %convolution_convert_fusion.4), channel_id=1, replica_groups=mesh['req'=8,'kv'=16] {'kv'}, dimensions={0}, use_global_device_ids=true | all-gather | bytes 417792 | tf_op jit(solution)/shard_map/all_gather | solution.py:187
  67.3 19.5 %all_gather.60 = bf16[128,1536]{1,0:T(8,128)(2,1)S(1)} all-gather(bf16[8,1536]{1,0:T(8,128)(2,1)S(1)} %convolution_convert_fusion.7), channel_id=1, replica_groups=mesh['req'=8,'kv'=16] {'kv'}, dimensions={0}, use_global_device_ids=true | all-gather | bytes 417792 | tf_op jit(solution)/shard_map/all_gather | solution.py:187
  96.4 17.5 %all_gather.65 = bf16[128,1536]{1,0:T(8,128)(2,1)S(1)} all-gather(bf16[8,1536]{1,0:T(8,128)(2,1)S(1)} %convolution_convert_fusion.6), channel_id=1, replica_groups=mesh['req'=8,'kv'=16] {'kv'}, dimensions={0}, use_global_device_ids=true | all-gather | bytes 417792 | tf_op jit(solution)/shard_map/all_gather | solution.py:187
  125.4 21.0 %all_gather.64 = bf16[128,256]{1,0:T(8,128)(2,1)S(1)} all-gather(bf16[8,256]{1,0:T(8,128)(2,1)S(1)} %convolution_convert_fusion.11), channel_id=1, replica_groups=mesh['req'=8,'kv'=16] {'kv'}, dimensions={0}, use_global_device_ids=true | all-gather | bytes 69632 | tf_op jit(solution)/shard_map/all_gather | solution.py:188
  149.3 16.8 %all_gather.69 = bf16[128,256]{1,0:T(8,128)(2,1)S(1)} all-gather(bf16[8,256]{1,0:T(8,128)(2,1)S(1)} %convolution_convert_fusion.10), channel_id=1, replica_groups=mesh['req'=8,'kv'=16] {'kv'}, dimensions={0}, use_global_device_ids=true | all-gather | bytes 69632 | tf_op jit(solution)/shard_map/all_gather | solution.py:188
  169.0 19.5 %all_gather.74 = bf16[128,256]{1,0:T(8,128)(2,1)S(1)} all-gather(bf16[8,256]{1,0:T(8,128)(2,1)S(1)} %convolution_convert_fusion.9), channel_id=1, replica_groups=mesh['req'=8,'kv'=16] {'kv'}, dimensions={0}, use_global_device_ids=true | all-gather | bytes 69632 | tf_op jit(solution)/shard_map/all_gather | solution.py:188
  191.5 16.5 %all_gather.79 = bf16[128,256]{1,0:T(8,128)(2,1)S(1)} all-gather(bf16[8,256]{1,0:T(8,128)(2,1)S(1)} %convolution_convert_fusion.8), channel_id=1, replica_groups=mesh['req'=8,'kv'=16] {'kv'}, dimensions={0}, use_global_device_ids=true | all-gather | bytes 69632 | tf_op jit(solution)/shard_map/all_gather | solution.py:188
  218.9 22.1 %all_gather.70 = bf16[128,1536]{1,0:T(8,128)(2,1)S(1)} all-gather(bf16[8,1536]{1,0:T(8,128)(2,1)S(1)} %convolution_convert_fusion.5), channel_id=1, replica_groups=mesh['req'=8,'kv'=16] {'kv'}, dimensions={0}, use_global_device_ids=true | all-gather | bytes 417792 | tf_op jit(solution)/shard_map/all_gather | solution.py:187
  248.9 19.9 %all_gather.76 = f32[16,16,8,12]{1,2,3,0:T(8,128)} all-gather(f32[1,16,8,12]{1,2,3,0:T(8,128)S(1)} %copy.375), channel_id=1, replica_groups=mesh['req'=8,'kv'=16] {'kv'}, dimensions={0}, use_global_device_ids=true | all-gather | bytes 104448 | tf_op jit(solution)/shard_map/all_gather | solution.py:36
  268.8 22.6 %all_gather.77 = f32[16,16,8,12]{1,2,3,0:T(8,128)} all-gather(f32[1,16,8,12]{1,2,3,0:T(8,128)S(1)} %copy.378), channel_id=1, replica_groups=mesh['req'=8,'kv'=16] {'kv'}, dimensions={0}, use_global_device_ids=true | all-gather | bytes 104448 | tf_op jit(solution)/shard_map/all_gather | solution.py:36
  291.4 20.6 %all_gather.61 = f32[16,16,8,12]{1,2,3,0:T(8,128)S(1)} all-gather(f32[1,16,8,12]{1,2,3,0:T(8,128)S(1)} %copy.320), channel_id=1, replica_groups=mesh['req'=8,'kv'=16] {'kv'}, dimensions={0}, use_global_device_ids=true | all-gather | bytes 104448 | tf_op jit(solution)/shard_map/all_gather | solution.py:36
  312.0 22.9 %all_gather.62 = f32[16,16,8,12]{1,2,3,0:T(8,128)S(1)} all-gather(f32[1,16,8,12]{1,2,3,0:T(8,128)S(1)} %copy.323), channel_id=1, replica_groups=mesh['req'=8,'kv'=16] {'kv'}, dimensions={0}, use_global_device_ids=true | all-gather | bytes 104448 | tf_op jit(solution)/shard_map/all_gather | solution.py:36
  334.9 21.5 %all_gather.66 = f32[16,16,8,12]{1,2,3,0:T(8,128)S(1)} all-gather(f32[1,16,8,12]{1,2,3,0:T(8,128)S(1)} %copy.341), channel_id=1, replica_groups=mesh['req'=8,'kv'=16] {'kv'}, dimensions={0}, use_global_device_ids=true | all-gather | bytes 104448 | tf_op jit(solution)/shard_map/all_gather | solution.py:36
  356.3 18.0 %all_gather.67 = f32[16,16,8,12]{1,2,3,0:T(8,128)S(1)} all-gather(f32[1,16,8,12]{1,2,3,0:T(8,128)S(1)} %copy.344), channel_id=1, replica_groups=mesh['req'=8,'kv'=16] {'kv'}, dimensions={0}, use_global_device_ids=true | all-gather | bytes 104448 | tf_op jit(solution)/shard_map/all_gather | solution.py:36
  374.3 19.6 %all_gather.71 = f32[16,16,8,12]{1,2,3,0:T(8,128)} all-gather(f32[1,16,8,12]{1,2,3,0:T(8,128)S(1)} %copy.358), channel_id=1, replica_groups=mesh['req'=8,'kv'=16] {'kv'}, dimensions={0}, use_global_device_ids=true | all-gather | bytes 104448 | tf_op jit(solution)/shard_map/all_gather | solution.py:36
  393.9 19.8 %all_gather.72 = f32[16,16,8,12]{1,2,3,0:T(8,128)} all-gather(f32[1,16,8,12]{1,2,3,0:T(8,128)S(1)} %copy.361), channel_id=1, replica_groups=mesh['req'=8,'kv'=16] {'kv'}, dimensions={0}, use_global_device_ids=true | all-gather | bytes 104448 | tf_op jit(solution)/shard_map/all_gather | solution.py:36
  426.2 46.2 %while.83 = (s32[]{:T(128)}, f32[16,8,12]{0,1,2:T(8,128)S(1)}, f32[16,8,12]{0,1,2:T(8,128)S(1)}, f32[16,8,12,128]{3,2,1,0:T(8,128)S(1)}, f32[16,16,8,12]{1,2,3,0...) while((s32[]{:T(128)}, f32[16,8,12]{0,1,2:T(8,128)S(1)}, ...), condition=%wide.region_32.33_spmd, body=%wide.region_31.32_spmd.sunk | while | flops 599045 | bytes 4018327 | solution.py:42
  474.8 46.3 %while.80 = (s32[]{:T(128)}, f32[16,8,12]{0,1,2:T(8,128)S(1)}, f32[16,8,12]{0,1,2:T(8,128)S(1)}, f32[16,8,12,128]{3,2,1,0:T(8,128)S(1)}, f32[16,16,8,12]{1,2,3,0...) while((s32[]{:T(128)}, f32[16,8,12]{0,1,2:T(8,128)S(1)}, ...), condition=%wide.region_7.8_spmd, body=%wide.region_6.7_spmd.sunk | while | flops 599045 | bytes 4018327 | solution.py:42
  524.0 73.3 %while.81 = (s32[]{:T(128)}, f32[16,8,12]{0,1,2:T(8,128)S(1)}, f32[16,8,12]{0,1,2:T(8,128)S(1)}, f32[16,8,12,128]{3,2,1,0:T(8,128)}, f32[16,16,8,12]{1,2,3,0:T(8...) while((s32[]{:T(128)}, f32[16,8,12]{0,1,2:T(8,128)S(1)}, ...), condition=%wide.region_14.15_spmd, body=%wide.region_13.14_spmd.sunk | while | flops 599045 | bytes 4018327 | solution.py:42
  609.4 46.2 %while.82 = (s32[]{:T(128)}, f32[16,8,12]{0,1,2:T(8,128)S(1)}, f32[16,8,12]{0,1,2:T(8,128)S(1)}, f32[16,8,12,128]{3,2,1,0:T(8,128)S(1)}, f32[16,16,8,12]{1,2,3,0...) while((s32[]{:T(128)}, f32[16,8,12]{0,1,2:T(8,128)S(1)}, ...), condition=%wide.region_23.24_spmd, body=%wide.region_22.23_spmd.sunk | while | flops 599045 | bytes 4018327 | solution.py:42
  839.2 169.4 %all-reduce.7.cloned.1.call-done = (bf16[128,1536]{1,0:T(8,128)(2,1)}, bf16[128,1536]{1,0:T(8,128)(2,1)}, bf16[128,1536]{1,0:T(8,128)(2,1)}, bf16[128,1536]{1,0:T(8,128)(2,1)}) async-done(((bf16[128,1536]{1,0:T(8,128)(2,1)}, bf16[128,1536]{1,0:T(8,128)(2,1)}, bf16[128,1536]{1,0:T(8,128)(2,1)}, bf16[128,1536]{1,0:T(8,128)(2,1)}), (bf16[128,1536]{1,0:T(8,128)(2,1)}, bf16[128,1536]{1,0:T(8,128)(2,1)}, ...) | async-done | bytes 1572880
  1012.9 6.5 all-to-all-start.1
  (894 shorter events, 507.3 us)
Async XLA Ops:
  12.5 22.6 %all-to-all-start = ((bf16[4,8,1,1536]{3,0,2,1:T(4,128)(2,1)}), bf16[4,8,1,1536]{3,0,2,1:T(4,128)(2,1)S(1)}, u32[]{:S(2)}, u32[]{:S(2)}) async-start(bf16[4,8,1,1536]{3,0,2,1:T(4,128)(2,1)} %copy.313), calls=%async_computation | async-start | bytes 196608 | tf_op jit(solution)/shard_map/all_to_all | solution.py:161
  18.3 406.6 %all-gather.11.cloned.1.call-start = ((), (), s32[]{:S(2)}) async-start(), calls=%async_computation.5 | async-start | bytes 13369344 | tf_op jit(solution)/shard_map/all_gather | solution.py:36
  64.0 408.7 %all-gather.5.cloned.1.call-start = ((), (), s32[]{:S(2)}) async-start(), calls=%async_computation.2 | async-start | bytes 13369344 | tf_op jit(solution)/shard_map/all_gather | solution.py:36
  93.0 428.7 %all-gather.7.cloned.1.call-start = ((), (), s32[]{:S(2)}) async-start(), calls=%async_computation.3 | async-start | bytes 13369344 | tf_op jit(solution)/shard_map/all_gather | solution.py:36
  120.2 487.8 %all-gather.9.cloned.1.call-start = ((), (), s32[]{:S(2)}) async-start(), calls=%async_computation.4 | async-start | bytes 13369344 | tf_op jit(solution)/shard_map/all_gather | solution.py:36
  424.0 584.5 %all-reduce.7.cloned.1.call-start = ((), (), s32[]{:S(2)}) async-start(), calls=%async_computation.6 | async-start | bytes 3145728
  696.7 12.2 %collective-permute-start.36 = (bf16[8,1536]{1,0:T(8,128)(2,1)S(1)}, bf16[8,1536]{1,0:T(8,128)(2,1)S(1)}, u32[]{:S(2)}, u32[]{:S(2)}) collective-permute-start(bf16[8,1536]{1,0:T(8,128)(2,1)S(1)} %collective-permute-done.35), channel_id=1, source_target_pairs={{0,1},{1,2},{2,3},{3,4},{4,5},{5,6},{6,7},{7,8},{8,9},{9,10},{10,1... | collective-permute-start | bytes 73736 | tf_op jit(solution)/shard_map/ppermute | solution.py:26
  702.4 10.0 collective-permute-start.52
  702.4 16.0 %collective-permute-start.53 = (bf16[8,1536]{1,0:T(8,128)(2,1)S(1)}, bf16[8,1536]{1,0:T(8,128)(2,1)S(1)}, u32[]{:S(2)}, u32[]{:S(2)}) collective-permute-start(bf16[8,1536]{1,0:T(8,128)(2,1)S(1)} %get-tuple-element.991), channel_id=1, source_target_pairs={{1,0},{2,1},{3,2},{4,3},{5,4},{6,5},{7,6},{8,7},{9,8},{10,9},{11,1... | collective-permute-start | bytes 73736 | tf_op jit(solution)/shard_map/ppermute | solution.py:28
  707.5 15.8 %collective-permute-start.38 = (bf16[8,1536]{1,0:T(8,128)(2,1)S(1)}, bf16[8,1536]{1,0:T(8,128)(2,1)S(1)}, u32[]{:S(2)}, u32[]{:S(2)}) collective-permute-start(bf16[8,1536]{1,0:T(8,128)(2,1)S(1)} %get-tuple-element.990), channel_id=1, source_target_pairs={{1,0},{2,1},{3,2},{4,3},{5,4},{6,5},{7,6},{8,7},{9,8},{10,9},{11,1... | collective-permute-start | bytes 73736 | tf_op jit(solution)/shard_map/ppermute | solution.py:28
  707.6 15.9 %collective-permute-start.15 = (bf16[8,1536]{1,0:T(8,128)(2,1)S(1)}, bf16[8,1536]{1,0:T(8,128)(2,1)S(1)}, u32[]{:S(2)}, u32[]{:S(2)}) collective-permute-start(bf16[8,1536]{1,0:T(8,128)(2,1)S(1)} %get-tuple-element.989), channel_id=1, source_target_pairs={{0,1},{1,2},{2,3},{3,4},{4,5},{5,6},{6,7},{7,8},{8,9},{9,10},{10,1... | collective-permute-start | bytes 73736 | tf_op jit(solution)/shard_map/ppermute | solution.py:26
  709.0 14.6 %collective-permute-start.23 = (bf16[8,1536]{1,0:T(8,128)(2,1)S(1)}, bf16[8,1536]{1,0:T(8,128)(2,1)S(1)}, u32[]{:S(2)}, u32[]{:S(2)}) collective-permute-start(bf16[8,1536]{1,0:T(8,128)(2,1)S(1)} %get-tuple-element.989), channel_id=1, source_target_pairs={{1,0},{2,1},{3,2},{4,3},{5,4},{6,5},{7,6},{8,7},{9,8},{10,9},{11,1... | collective-permute-start | bytes 73736 | tf_op jit(solution)/shard_map/ppermute | solution.py:28
  718.5 9.9 collective-permute-start.8
  728.4 9.8 collective-permute-start.9
  738.3 9.8 collective-permute-start.10
  748.1 9.8 collective-permute-start.11
  753.1 10.0 collective-permute-start.19
  758.0 10.1 collective-permute-start.12
  764.7 10.5 %collective-permute-start.28 = (bf16[8,1536]{1,0:T(8,128)(2,1)S(1)}, bf16[8,1536]{1,0:T(8,128)(2,1)}, u32[]{:S(2)}, u32[]{:S(2)}) collective-permute-start(bf16[8,1536]{1,0:T(8,128)(2,1)S(1)} %collective-permute-done.27), channel_id=1, source_target_pairs={{1,0},{2,1},{3,2},{4,3},{5,4},{6,5},{7,6},{8,7},{9,8},{10,9},{11,1... | collective-permute-start | bytes 73736 | tf_op jit(solution)/shard_map/ppermute | solution.py:28
  768.1 11.8 %collective-permute-start.13 = (bf16[8,1536]{1,0:T(8,128)(2,1)S(1)}, bf16[8,1536]{1,0:T(8,128)(2,1)}, u32[]{:S(2)}, u32[]{:S(2)}) collective-permute-start(bf16[8,1536]{1,0:T(8,128)(2,1)S(1)} %collective-permute-done.12), channel_id=1, source_target_pairs={{1,0},{2,1},{3,2},{4,3},{5,4},{6,5},{7,6},{8,7},{9,8},{10,9},{11,1... | collective-permute-start | bytes 73736 | tf_op jit(solution)/shard_map/ppermute | solution.py:28
  779.9 34.7 %collective-permute-start.29 = (bf16[8,1536]{1,0:T(8,128)(2,1)}, bf16[8,1536]{1,0:T(8,128)(2,1)}, u32[]{:S(2)}, u32[]{:S(2)}) collective-permute-start(bf16[8,1536]{1,0:T(8,128)(2,1)} %collective-permute-done.28), channel_id=1, source_target_pairs={{1,0},{2,1},{3,2},{4,3},{5,4},{6,5},{7,6},{8,7},{9,8},{10,9},{11,1... | collective-permute-start | bytes 73736 | tf_op jit(solution)/shard_map/ppermute | solution.py:28
  780.0 52.6 %collective-permute-start.14 = (bf16[8,1536]{1,0:T(8,128)(2,1)}, bf16[8,1536]{1,0:T(8,128)(2,1)}, u32[]{:S(2)}, u32[]{:S(2)}) collective-permute-start(bf16[8,1536]{1,0:T(8,128)(2,1)} %collective-permute-done.13), channel_id=1, source_target_pairs={{1,0},{2,1},{3,2},{4,3},{5,4},{6,5},{7,6},{8,7},{9,8},{10,9},{11,1... | collective-permute-start | bytes 73736 | tf_op jit(solution)/shard_map/ppermute | solution.py:28
  781.5 36.4 %collective-permute-start.7 = (bf16[8,1536]{1,0:T(8,128)(2,1)}, bf16[8,1536]{1,0:T(8,128)(2,1)}, u32[]{:S(2)}, u32[]{:S(2)}) collective-permute-start(bf16[8,1536]{1,0:T(8,128)(2,1)} %collective-permute-done.6), channel_id=1, source_target_pairs={{0,1},{1,2},{2,3},{3,4},{4,5},{5,6},{6,7},{7,8},{8,9},{9,10},{10,1... | collective-permute-start | bytes 73736 | tf_op jit(solution)/shard_map/ppermute | solution.py:26
  1012.9 11.4 %all-to-all-start.1 = ((bf16[4,8,1,1536]{3,0,2,1:T(4,128)(2,1)}), bf16[4,8,1,1536]{3,0,2,1:T(4,128)(2,1)S(1)}, u32[]{:S(2)}, u32[]{:S(2)}) async-start(bf16[4,8,1,1536]{3,0,2,1:T(4,128)(2,1)} %bitcast.209), calls=%async_computation.1 | async-start | bytes 196608 | tf_op jit(solution)/shard_map/all_to_all | solution.py:227
  (129 other events, 4751.1 us)
Sparse Core Ops, SparseCore 0:
  64.1 97.4 all-gather.10
  163.7 91.9 all-gather.4
  258.0 102.0 all-gather.6
  424.1 153.2 all-gather.8
  838.0 170.5 all-reduce.6
